TPU v7x, 256 devices: a whole 4x4x8 slice. The times are simulated.
256 devices in a mesh: dp: 16 (over y, x), expert: 16 (over z, core).
Axes of the slice: x: 4, y: 4, z: 8, core: 2. Of those that a mesh axis runs over, the one named last changes fastest.
Arguments:
- tokens: bfloat16 [32768, 768], P(('dp', 'expert')), may hold values from -24 to 24
- expert_ids: int32 [32768, 2], P(('dp', 'expert')), may hold values from 0 to 15, all different within a row; in each aligned block of 128 rows (0 to 127, 128 to 255, ...) at most 32 rows name the same one
- router: bfloat16 [768, 16], replicated, may hold values from -0.4375 to 0.4375
- weight_in: bfloat16 [16, 768, 3072], P('expert'), may hold values from -0.21875 to 0.21875
- weight_out: bfloat16 [16, 3072, 768], P('expert'), may hold values from -0.4375 to 0.4375
- premises: bfloat16 [2048, 768], P('dp'), may hold values from -6 to 6
- positive: int32 [512], replicated, may hold values from 0 to 2047
- tile_mask: int32 [256, 16], replicated, may hold values 0 or 1
Outputs:
- grad_in: float32 [16, 768, 3072], P('expert', 'dp')
- grad_out: float32 [16, 3072, 768], P('expert', 'dp')
Inputs may be any that keep to these rules, and one draw needn't show every extreme that they name: `expert_ids`: among the 128 tokens of one device no expert is named by more than 32 pairs, and one expert is named by exactly 32; the two experts of a token differ.
All inputs are finite; a program needn't handle non-finite values.
Results may differ from a plain program's by a relative error of at most 0.02.
Values may be sent and summed in bfloat16 or wider, within the bound.
No kernel may reach another device: no remote copies, remote signals or barrier semaphores. Data moves between devices by JAX's collectives and lax.ppermute only.
A program may use at most 128 MiB of HBM per device.

v0:
```python
import jax
import jax.numpy as jnp
from jax import lax
from jax.sharding import PartitionSpec as P

LEN = 64


SCORE_SCALE = 20.0
LOSS_SCALE = 64.0
EPSILON = 1e-06


def gelu_parts(pre_act):
    inner_arg = 0.7978845608028654 * (pre_act + 0.044715 * pre_act * pre_act * pre_act)
    tangent = jnp.tanh(inner_arg)
    gelu_val = 0.5 * pre_act * (1.0 + tangent)
    slope_val = 0.5 * (1.0 + tangent) + 0.5 * pre_act * (
        1.0 - tangent * tangent
    ) * 0.7978845608028654 * (1.0 + 0.134145 * pre_act * pre_act)
    return (gelu_val, slope_val)


def route_slots(expert_ids, logits, experts, capacity):
    pick_hot = expert_ids[:, :, None] == jnp.arange(experts, dtype=jnp.int32)[None, None, :]
    picked = jnp.sum(jnp.where(pick_hot, logits[:, None, :], jnp.zeros((), logits.dtype)), axis=2)
    gate_wts = jax.nn.sigmoid(picked - picked[:, ::-1]).astype(jnp.bfloat16)
    flat_ids = expert_ids.reshape(-1)
    flat_hot = (flat_ids[:, None] == jnp.arange(experts, dtype=jnp.int32)[None, :]).astype(
        jnp.int32
    )
    running = jnp.cumsum(flat_hot, axis=0)
    position = jnp.sum(running * flat_hot, axis=1) - 1
    slot_ids = flat_ids * capacity + position
    return (gate_wts, slot_ids.reshape(expert_ids.shape))


def contrast_terms(query_vec, key_rows, key_scale, open_mask, pos_hot):
    include = jnp.logical_or(open_mask, pos_hot)
    scores = (
        SCORE_SCALE
        * lax.dot_general(
            query_vec, key_rows, (((1,), (1,)), ((), ())), preferred_element_type=jnp.float32
        )
        * key_scale[None, :]
    )
    exp_scores = jnp.where(include, jnp.exp(scores), jnp.zeros((), scores.dtype))
    partition = jnp.sum(exp_scores, axis=1)
    soft_weight = (exp_scores * key_scale[None, :]).astype(jnp.bfloat16)
    weighted_sum = jnp.dot(soft_weight, key_rows, preferred_element_type=jnp.float32)
    pos_scale = jnp.sum(
        jnp.where(pos_hot, key_scale[None, :], jnp.zeros((), key_scale.dtype)), axis=1
    )
    pos_vec = (
        jnp.dot(pos_hot.astype(jnp.bfloat16), key_rows, preferred_element_type=jnp.float32)
        * pos_scale[:, None]
    )
    return (weighted_sum, partition, pos_vec)


def on_device(tokens, expert_ids, router, weight_in, weight_out, premises, positive, tile_mask):
    token_count, model_width = tokens.shape
    ffn_width = weight_in.shape[2]
    experts = router.shape[1]
    expert_size = lax.axis_size("expert")
    capacity = 4 * token_count // expert_size
    slot_total = experts * capacity
    dp_index = lax.axis_index("dp")
    col_index = lax.axis_index("expert")
    device = dp_index * expert_size + col_index
    logits = jnp.dot(tokens, router, preferred_element_type=jnp.float32)
    gate_wts, slot_ids = route_slots(expert_ids, logits, experts, capacity)
    slot_hot = slot_ids[:, :, None] == jnp.arange(slot_total, dtype=jnp.int32)[None, None, :]
    placing = jnp.sum(slot_hot.astype(jnp.bfloat16), axis=1)
    combine = jnp.sum(
        jnp.where(slot_hot, gate_wts[:, :, None], jnp.zeros((), jnp.bfloat16)), axis=1
    )
    outgoing = lax.dot_general(
        placing, tokens, (((0,), (0,)), ((), ())), preferred_element_type=jnp.float32
    ).astype(jnp.bfloat16)
    outgoing = outgoing.reshape(experts, capacity, model_width)
    arrived = lax.all_to_all(outgoing, "expert", split_axis=0, concat_axis=0, tiled=True)
    sources = arrived.shape[0]
    slot_count = arrived.shape[1]
    flat_in = arrived.reshape(sources * slot_count, model_width)
    pre_act = jnp.dot(flat_in, weight_in[0], preferred_element_type=jnp.float32)
    gelu_val, slope_val = gelu_parts(pre_act)
    hidden = gelu_val.astype(jnp.bfloat16)
    result = jnp.dot(hidden, weight_out[0], preferred_element_type=jnp.float32).astype(jnp.bfloat16)
    returned = lax.all_to_all(
        result.reshape(sources, slot_count, model_width),
        "expert",
        split_axis=0,
        concat_axis=0,
        tiled=True,
    )
    received, hidden, slope_val, returned = (
        arrived,
        hidden.reshape(sources, slot_count, ffn_width),
        slope_val.reshape(sources, slot_count, ffn_width),
        returned,
    )
    mixed_out = tokens.astype(jnp.float32) + jnp.dot(
        combine, returned.reshape(slot_total, model_width), preferred_element_type=jnp.float32
    )
    seq_count = token_count // LEN
    pooled = jnp.sum(mixed_out.reshape(seq_count, LEN, model_width), axis=1) / LEN
    row_scale = lax.rsqrt(jnp.sum(pooled * pooled, axis=1) + EPSILON)
    unit_vec = pooled * row_scale[:, None]
    query_vec = unit_vec.astype(jnp.bfloat16)
    prem_count = premises.shape[0]
    key_rows = lax.all_gather(premises, "dp", axis=0, tiled=True)
    key_scale = lax.rsqrt(jnp.sum(jnp.square(key_rows.astype(jnp.float32)), axis=1) + EPSILON)
    key_index = jnp.arange(key_rows.shape[0], dtype=jnp.int32)
    own_positive = lax.dynamic_slice_in_dim(positive, device * seq_count, seq_count)
    mask_row = lax.dynamic_index_in_dim(tile_mask, device, 0, keepdims=False)
    key_open = jnp.repeat(mask_row, prem_count) == 1
    weighted_sum, partition, pos_vec = contrast_terms(
        query_vec,
        key_rows,
        key_scale,
        key_open[None, :],
        key_index[None, :] == own_positive[:, None],
    )
    delta_unit = LOSS_SCALE * SCORE_SCALE * (weighted_sum / partition[:, None] - pos_vec)
    delta_pooled = row_scale[:, None] * (
        delta_unit - unit_vec * jnp.sum(unit_vec * delta_unit, axis=1, keepdims=True)
    )
    delta_mixed = jnp.broadcast_to(
        delta_pooled[:, None, :] / LEN, (seq_count, LEN, model_width)
    ).reshape(token_count, model_width)
    grad_send = lax.dot_general(
        combine.astype(jnp.float32),
        delta_mixed,
        (((0,), (0,)), ((), ())),
        precision=lax.Precision.HIGHEST,
        preferred_element_type=jnp.float32,
    ).astype(jnp.bfloat16)
    grad_recv = lax.all_to_all(
        grad_send.reshape(experts, capacity, model_width),
        "expert",
        split_axis=0,
        concat_axis=0,
        tiled=True,
    )
    grad_flat = grad_recv.reshape(-1, model_width)
    row_total = grad_flat.shape[0]
    hidden_flat = hidden.reshape(row_total, ffn_width)
    slope_flat = slope_val.reshape(row_total, ffn_width)
    input_flat = received.reshape(row_total, model_width)
    grad_out_term = lax.dot_general(
        hidden_flat, grad_flat, (((0,), (0,)), ((), ())), preferred_element_type=jnp.float32
    )
    dhidden = lax.dot_general(
        grad_flat, weight_out[0], (((1,), (1,)), ((), ())), preferred_element_type=jnp.float32
    )
    delta_pre = (dhidden * slope_flat).astype(jnp.bfloat16)
    grad_in_term = lax.dot_general(
        input_flat, delta_pre, (((0,), (0,)), ((), ())), preferred_element_type=jnp.float32
    )
    grad_in, grad_out = (
        lax.psum_scatter(
            grad_in_term[None].astype(jnp.bfloat16), "dp", scatter_dimension=1, tiled=True
        ).astype(jnp.float32),
        lax.psum_scatter(
            grad_out_term[None].astype(jnp.bfloat16), "dp", scatter_dimension=1, tiled=True
        ).astype(jnp.float32),
    )
    return (grad_in, grad_out)


def solution(mesh):
    in_specs = (
        P(("dp", "expert"), None),
        P(("dp", "expert"), None),
        P(),
        P("expert", None, None),
        P("expert", None, None),
        P("dp", None),
        P(),
        P(),
    )
    out_specs = (P("expert", "dp", None), P("expert", "dp", None))
    return jax.shard_map(
        on_device, mesh=mesh, in_specs=in_specs, out_specs=out_specs, check_vma=False
    )
```

profile of v0, /device:TPU:32, one launch (start us, length us, event | category | flops | bytes accessed | tf_op | source)
XLA Modules:
  0.0 303.2 jit_solution(11562234497261037205)
XLA Ops:
  7.2 0.0 copy-start
  7.2 0.0 all-gather.2.cloned.1.call-start
  7.2 0.7 all-gather.2.cloned.1.call-update
  7.9 0.8 copy.26
  8.7 0.1 eq.81
  8.8 0.1 eq.85
  9.0 0.6 reduce-window.6
  9.6 0.2 slice_reduce_fusion
  9.8 0.1 fusion.28
  9.9 0.1 sub.19
  10.1 0.1 copy.29
  10.1 0.0 copy-done
  10.1 1.1 fusion.40
  11.2 0.8 select_reduce_fusion.1
  12.0 0.7 multiply_add_fusion.1
  12.7 0.2 fusion.26
  12.9 1.3 convolution_convert_fusion.3
  14.2 29.4 %all_to_all.15 = bf16[16,32,768]{2,1,0:T(8,128)(2,1)S(1)} all-to-all(bf16[16,32,768]{2,1,0:T(8,128)(2,1)S(1)} %bitcast.61), channel_id=1, replica_groups=mesh['dp'=16,'expert'=16] {'expert'}, dimensions={0} | all-to-all | bytes 1572864 | tf_op jit(solution)/shard_map/all_to_all | solution.py:82
  43.6 4.6 %fusion.10 = f32[512,3072]{1,0:T(8,128)S(1)} fusion(bf16[512,768]{1,0:T(8,128)(2,1)S(1)} %bitcast.57, bf16[1,768,3072]{2,1,0:T(8,128)(2,1)} %param.11), kind=kOutput, calls=%fused_computation.16 | convolution fusion | flops 2415919104 | bytes 11796480 | tf_op jit(solution)/shard_map/dot_general | solution.py:86
  48.2 0.0 copy-start.4
  48.2 0.0 copy-start.3
  48.2 4.7 %fusion.18 = bf16[512,768]{1,0:T(8,128)(2,1)} fusion(bf16[1,3072,768]{2,1,0:T(8,128)(2,1)S(1)} %bitcast.66, f32[512,3072]{1,0:T(8,128)S(1)} %fusion.10), kind=kOutput, calls=%fused_computation.23 | convolution fusion | flops 2430468096 | bytes 11796480 | tf_op jit(solution)/shard_map/dot_general | solution.py:89
  53.0 4.9 %all-to-all-start.1 = ((bf16[16,32,768]{2,1,0:T(8,128)(2,1)}), bf16[16,32,768]{2,1,0:T(8,128)(2,1)S(1)}, u32[]{:S(2)}, u32[]{:S(2)}) async-start(bf16[16,32,768]{2,1,0:T(8,128)(2,1)} %bitcast.5), calls=%async_computation.1 | async-start | bytes 1572864 | tf_op jit(solution)/shard_map/all_to_all | solution.py:90
  57.8 0.0 reduce-scatter.3.cloned.1.call-start
  57.9 0.8 dynamic_slice.8
  58.7 0.2 fusion.32
  58.8 0.1 broadcast_bitcast_fusion
  58.9 18.0 %all-to-all-done.1 = bf16[16,32,768]{2,1,0:T(8,128)(2,1)S(1)} async-done(((bf16[16,32,768]{2,1,0:T(8,128)(2,1)}), bf16[16,32,768]{2,1,0:T(8,128)(2,1)S(1)}, u32[]{:S(2)}, u32[]{:S(2)}) %all-to-all-start.1) | async-done | bytes 786464 | tf_op jit(solution)/shard_map/all_to_all | solution.py:90
  76.9 0.3 bitcast_reduce_fusion
  77.2 0.1 multiply_reduce_fusion.2
  77.4 0.0 all-gather.2.cloned.1.call-done
  77.4 2.7 multiply_reduce_fusion
  80.1 0.2 select_reduce_fusion
  80.3 2.9 fusion.39
  83.3 0.5 convolution_divide_fusion
  83.8 0.7 multiply_reduce_fusion.1
  84.5 0.1 multiply_multiply_fusion.1
  84.6 0.8 convolution_convert_fusion.2
  85.4 27.5 %all_to_all.16 = bf16[16,32,768]{2,1,0:T(8,128)(2,1)S(1)} all-to-all(bf16[16,32,768]{2,1,0:T(8,128)(2,1)S(1)} %bitcast.60), channel_id=1, replica_groups=mesh['dp'=16,'expert'=16] {'expert'}, dimensions={0} | all-to-all | bytes 1572864 | tf_op jit(solution)/shard_map/all_to_all | solution.py:139
  113.0 11.4 %fusion.12 = bf16[1,768,3072]{2,1,0:T(8,128)(2,1)} fusion(bf16[512,768]{1,0:T(8,128)(2,1)S(1)} %bitcast.58, f32[512,3072]{1,0:T(8,128)} %copy-done.2, bf16[512,768]{1,0:T(8,128)(2,1)S(1)} %bitcast.63, bf16[1,3072,768]{2,1,0:T(8,128)(2,1)} %param.12), kind=kOutput, calls=%fused_computation.18 | convolution fusion | flops 4864081920 | bytes 17301504 | tf_op jit(solution)/shard_map/dot_general | solution.py:158
  124.3 0.0 reduce-scatter.3.cloned.1.call-update
  124.4 0.2 reduce-scatter.5.cloned.1.call-start
  124.6 8.4 %fusion.13 = bf16[1,3072,768]{2,1,0:T(8,128)(2,1)} fusion(bf16[512,768]{1,0:T(8,128)(2,1)S(1)} %bitcast.64, f32[512,3072]{1,0:T(8,128)} %copy-done.2), kind=kOutput, calls=%fused_computation.19 | convolution fusion | flops 2432434176 | bytes 11796480 | tf_op jit(solution)/shard_map/dot_general | solution.py:151
  133.0 0.0 reduce-scatter.5.cloned.1.call-update
  133.0 74.7 %reduce-scatter.3.cloned.1.call-done = bf16[1,48,3072]{2,1,0:T(8,128)(2,1)} async-done(((bf16[1,768,3072]{2,1,0:T(8,128)(2,1)}), bf16[1,48,3072]{2,1,0:T(8,128)(2,1)}) %reduce-scatter.3.cloned.1.call-update) | async-done | bytes 294928 | tf_op jit(solution)/shard_map/reduce_scatter | solution.py:162
  207.7 1.8 convert_element_type.76
  209.5 85.4 %reduce-scatter.5.cloned.1.call-done = bf16[1,192,768]{2,1,0:T(8,128)(2,1)} async-done(((bf16[1,3072,768]{2,1,0:T(8,128)(2,1)}), bf16[1,192,768]{2,1,0:T(8,128)(2,1)}) %reduce-scatter.5.cloned.1.call-update) | async-done | bytes 294928 | tf_op jit(solution)/shard_map/reduce_scatter | solution.py:165
  294.9 1.8 convert_element_type.79
  (20 shorter events, 0.2 us)
Async XLA Ops:
  7.2 3.0 copy-start
  7.2 70.2 %all-gather.2.cloned.1.call-start = ((), (), s32[]{:S(2)}) async-start(), calls=%async_computation.5 | async-start | bytes 3342336 | tf_op jit(solution)/shard_map/all_gather | solution.py:112
  43.5 4.6 %slice-start = ((s8[4718592]{0:T(1024)(128)(4,1)}), s8[4194304]{0:T(1024)(128)(4,1)S(1)}, s32[]{:S(2)}) async-start(s8[4718592]{0:T(1024)(128)(4,1)} %bitcast.65), calls=%async_computation.8 | async-start | bytes 8388608
  43.6 4.6 %slice-start.1 = ((s8[4718592]{0:T(1024)(128)(4,1)}), s8[524288]{0:T(1024)(128)(4,1)S(1)}, s32[]{:S(2)}) async-start(s8[4718592]{0:T(1024)(128)(4,1)} %bitcast.65), calls=%async_computation.9 | async-start | bytes 1048576
  48.2 4.8 %copy-start.2 = (f32[512,3072]{1,0:T(8,128)}, f32[512,3072]{1,0:T(8,128)S(1)}, u32[]{:S(2)}) copy-start(f32[512,3072]{1,0:T(8,128)S(1)} %fusion.10) | copy-start | bytes 18874372
  48.2 10.4 %copy-start.4 = (s32[256,16]{0,1:T(8,128)S(1)}, s32[256,16]{0,1:T(8,128)}, u32[]{:S(2)}) copy-start(s32[256,16]{0,1:T(8,128)} %param.15) | copy-start | bytes 49156
  48.2 28.7 %copy-start.3 = (bf16[128,768]{1,0:T(8,128)(2,1)S(1)}, bf16[128,768]{1,0:T(8,128)(2,1)}, u32[]{:S(2)}) copy-start(bf16[128,768]{1,0:T(8,128)(2,1)} %param.8) | copy-start | bytes 589828
  53.0 24.0 %all-to-all-start.1 = ((bf16[16,32,768]{2,1,0:T(8,128)(2,1)}), bf16[16,32,768]{2,1,0:T(8,128)(2,1)S(1)}, u32[]{:S(2)}, u32[]{:S(2)}) async-start(bf16[16,32,768]{2,1,0:T(8,128)(2,1)} %bitcast.5), calls=%async_computation.1 | async-start | bytes 1572864 | tf_op jit(solution)/shard_map/all_to_all | solution.py:90
  57.8 149.8 %reduce-scatter.3.cloned.1.call-start = ((), (), s32[]{:S(2)}) async-start(), calls=%async_computation.6 | async-start | bytes 5013504 | tf_op jit(solution)/shard_map/reduce_scatter | solution.py:162
  77.4 5.9 %copy-start.1 = (bf16[2048,768]{1,0:T(8,128)(2,1)S(1)}, bf16[2048,768]{1,0:T(8,128)(2,1)}, u32[]{:S(2)}) copy-start(bf16[2048,768]{1,0:T(8,128)(2,1)} %all-gather.2.cloned.1.call-done) | copy-start | bytes 9437188
  124.4 170.5 %reduce-scatter.5.cloned.1.call-start = ((), (), s32[]{:S(2)}) async-start(), calls=%async_computation.7 | async-start | bytes 5013504 | tf_op jit(solution)/shard_map/reduce_scatter | solution.py:165
Sparse Core Ops, SparseCore 0:
  10.4 55.3 all-gather.1
  124.5 83.1 reduce-scatter.2
  211.3 83.4 reduce-scatter.4
where the time goes:
time: 304 us; the launch traced here: 303 us
  waiting for transfers between devices  179 us (59%)
  blocking collectives  56.9 us (19%)
  matrix products  36.7 us (12%)
  between operations  13.9 us (5%)
  other arithmetic  9.31 us (3%)
  starting transfers between devices  5.16 us (2%)
    reduce_scatter x1, waiting for transfers between devices, on_device(): lax.psum_scatter(grad_out_term[None].astype(jnp.bfloat16), 'dp', scatter_...  85.4 us
    reduce_scatter x1, waiting for transfers between devices, on_device(): lax.psum_scatter(grad_in_term[None].astype(jnp.bfloat16), 'dp', scatter_d...  74.7 us
    all_to_all x1, blocking collectives, on_device(): lax.all_to_all(outgoing, 'expert', split_axis=0, concat_axis=0, tiled=True)  29.4 us
    all_to_all x1, blocking collectives, on_device(): lax.all_to_all(grad_send.reshape(experts, capacity, model_width), 'expert...  27.5 us
    all_to_all x1, waiting for transfers between devices, on_device(): lax.all_to_all(result.reshape(sources, slot_count, model_width), 'expert'...  18 us
    dot_general x1, matrix products, on_device(): lax.dot_general(input_flat, delta_pre, (((0,), (0,)), ((), ())), preferre...  11.4 us
    dot_general x1, matrix products, on_device(): lax.dot_general(hidden_flat, grad_flat, (((0,), (0,)), ((), ())), preferr...  8.36 us
  transfers between devices with their start and end apart: 4, of which 3 were waited for; matrix products, arithmetic and copies ran while one was open for 9% of the time, Pallas kernels for 0%

commit v1 on v0

--- a/solution.py
+++ b/solution.py
@@ -9,6 +9,7 @@
 SCORE_SCALE = 20.0
 LOSS_SCALE = 64.0
 EPSILON = 1e-06
+HIGHEST = lax.Precision.HIGHEST
 
 
 def gelu_parts(pre_act):
@@ -33,6 +34,14 @@
     position = jnp.sum(running * flat_hot, axis=1) - 1
     slot_ids = flat_ids * capacity + position
     return (gate_wts, slot_ids.reshape(expert_ids.shape))
+
+
+def split_dot(a, b, dims):
+    a_hi = a.astype(jnp.bfloat16)
+    a_lo = (a - a_hi.astype(jnp.float32)).astype(jnp.bfloat16)
+    hi = lax.dot_general(a_hi, b, dims, preferred_element_type=jnp.float32)
+    lo = lax.dot_general(a_lo, b, dims, preferred_element_type=jnp.float32)
+    return hi + lo
 
 
 def contrast_terms(query_vec, key_rows, key_scale, open_mask, pos_hot):
@@ -63,11 +72,14 @@
     ffn_width = weight_in.shape[2]
     experts = router.shape[1]
     expert_size = lax.axis_size("expert")
+    dp_size = lax.axis_size("dp")
     capacity = 4 * token_count // expert_size
     slot_total = experts * capacity
+    seq_count = token_count // LEN
     dp_index = lax.axis_index("dp")
     col_index = lax.axis_index("expert")
     device = dp_index * expert_size + col_index
+
     logits = jnp.dot(tokens, router, preferred_element_type=jnp.float32)
     gate_wts, slot_ids = route_slots(expert_ids, logits, experts, capacity)
     slot_hot = slot_ids[:, :, None] == jnp.arange(slot_total, dtype=jnp.int32)[None, None, :]
@@ -75,36 +87,36 @@
     combine = jnp.sum(
         jnp.where(slot_hot, gate_wts[:, :, None], jnp.zeros((), jnp.bfloat16)), axis=1
     )
+    seq_hot = (
+        (jnp.arange(token_count, dtype=jnp.int32) // LEN)[:, None]
+        == jnp.arange(seq_count, dtype=jnp.int32)[None, :]
+    ).astype(jnp.float32)
+    slot_meta = lax.dot_general(
+        combine.astype(jnp.float32), seq_hot, (((0,), (0,)), ((), ())),
+        precision=HIGHEST, preferred_element_type=jnp.float32,
+    )
+    meta_all = lax.all_gather(slot_meta.reshape(experts, capacity, seq_count), "expert")
+    my_meta = lax.dynamic_index_in_dim(meta_all, col_index, 1, keepdims=False)
+    same_src = jnp.eye(expert_size, dtype=jnp.float32)
+    meta_t = jnp.transpose(my_meta, (2, 0, 1))
+    sel_gate = same_src[:, None, :, None] * meta_t[None, :, :, :]
+    sel_gate = sel_gate.reshape(expert_size * seq_count, expert_size * capacity)
+
     outgoing = lax.dot_general(
         placing, tokens, (((0,), (0,)), ((), ())), preferred_element_type=jnp.float32
     ).astype(jnp.bfloat16)
     outgoing = outgoing.reshape(experts, capacity, model_width)
     arrived = lax.all_to_all(outgoing, "expert", split_axis=0, concat_axis=0, tiled=True)
-    sources = arrived.shape[0]
-    slot_count = arrived.shape[1]
-    flat_in = arrived.reshape(sources * slot_count, model_width)
-    pre_act = jnp.dot(flat_in, weight_in[0], preferred_element_type=jnp.float32)
-    gelu_val, slope_val = gelu_parts(pre_act)
+    input_flat = arrived.reshape(expert_size * capacity, model_width)
+    pre_act = jnp.dot(input_flat, weight_in[0], preferred_element_type=jnp.float32)
+    gelu_val, slope_flat = gelu_parts(pre_act)
     hidden = gelu_val.astype(jnp.bfloat16)
-    result = jnp.dot(hidden, weight_out[0], preferred_element_type=jnp.float32).astype(jnp.bfloat16)
-    returned = lax.all_to_all(
-        result.reshape(sources, slot_count, model_width),
-        "expert",
-        split_axis=0,
-        concat_axis=0,
-        tiled=True,
-    )
-    received, hidden, slope_val, returned = (
-        arrived,
-        hidden.reshape(sources, slot_count, ffn_width),
-        slope_val.reshape(sources, slot_count, ffn_width),
-        returned,
-    )
-    mixed_out = tokens.astype(jnp.float32) + jnp.dot(
-        combine, returned.reshape(slot_total, model_width), preferred_element_type=jnp.float32
-    )
-    seq_count = token_count // LEN
-    pooled = jnp.sum(mixed_out.reshape(seq_count, LEN, model_width), axis=1) / LEN
+    seq_hidden = jnp.dot(sel_gate.astype(jnp.bfloat16), hidden, preferred_element_type=jnp.float32)
+    moe_seq = split_dot(seq_hidden, weight_out[0], (((1,), (0,)), ((), ())))
+    moe_mine = lax.psum_scatter(moe_seq, "expert", scatter_dimension=0, tiled=True)
+
+    token_sum = jnp.sum(tokens.astype(jnp.float32).reshape(seq_count, LEN, model_width), axis=1)
+    pooled = (token_sum + moe_mine) / LEN
     row_scale = lax.rsqrt(jnp.sum(pooled * pooled, axis=1) + EPSILON)
     unit_vec = pooled * row_scale[:, None]
     query_vec = unit_vec.astype(jnp.bfloat16)
@@ -126,31 +138,13 @@
     delta_pooled = row_scale[:, None] * (
         delta_unit - unit_vec * jnp.sum(unit_vec * delta_unit, axis=1, keepdims=True)
     )
-    delta_mixed = jnp.broadcast_to(
-        delta_pooled[:, None, :] / LEN, (seq_count, LEN, model_width)
-    ).reshape(token_count, model_width)
-    grad_send = lax.dot_general(
-        combine.astype(jnp.float32),
-        delta_mixed,
-        (((0,), (0,)), ((), ())),
-        precision=lax.Precision.HIGHEST,
-        preferred_element_type=jnp.float32,
+    delta_seq = delta_pooled / LEN
+    delta_row = lax.all_gather(delta_seq, "expert", axis=0, tiled=True)
+
+    grad_flat = lax.dot_general(
+        sel_gate, delta_row, (((0,), (0,)), ((), ())),
+        precision=HIGHEST, preferred_element_type=jnp.float32,
     ).astype(jnp.bfloat16)
-    grad_recv = lax.all_to_all(
-        grad_send.reshape(experts, capacity, model_width),
-        "expert",
-        split_axis=0,
-        concat_axis=0,
-        tiled=True,
-    )
-    grad_flat = grad_recv.reshape(-1, model_width)
-    row_total = grad_flat.shape[0]
-    hidden_flat = hidden.reshape(row_total, ffn_width)
-    slope_flat = slope_val.reshape(row_total, ffn_width)
-    input_flat = received.reshape(row_total, model_width)
-    grad_out_term = lax.dot_general(
-        hidden_flat, grad_flat, (((0,), (0,)), ((), ())), preferred_element_type=jnp.float32
-    )
     dhidden = lax.dot_general(
         grad_flat, weight_out[0], (((1,), (1,)), ((), ())), preferred_element_type=jnp.float32
     )
@@ -158,15 +152,19 @@
     grad_in_term = lax.dot_general(
         input_flat, delta_pre, (((0,), (0,)), ((), ())), preferred_element_type=jnp.float32
     )
-    grad_in, grad_out = (
-        lax.psum_scatter(
-            grad_in_term[None].astype(jnp.bfloat16), "dp", scatter_dimension=1, tiled=True
-        ).astype(jnp.float32),
-        lax.psum_scatter(
-            grad_out_term[None].astype(jnp.bfloat16), "dp", scatter_dimension=1, tiled=True
-        ).astype(jnp.float32),
+    grad_in = lax.psum_scatter(
+        grad_in_term[None].astype(jnp.bfloat16), "dp", scatter_dimension=1, tiled=True
+    ).astype(jnp.float32)
+
+    block = ffn_width // dp_size
+    hidden_blocks = jnp.transpose(
+        seq_hidden.reshape(expert_size * seq_count, dp_size, block), (1, 0, 2)
     )
-    return (grad_in, grad_out)
+    hidden_cols = lax.all_to_all(hidden_blocks, "dp", split_axis=0, concat_axis=0, tiled=True)
+    hidden_cols = hidden_cols.reshape(dp_size * expert_size * seq_count, block)
+    delta_all = lax.all_gather(delta_row.astype(jnp.bfloat16), "dp", axis=0, tiled=True)
+    grad_out = split_dot(hidden_cols, delta_all, (((0,), (0,)), ((), ())))
+    return (grad_in, grad_out[None])
 
 
 def solution(mesh):

time: 304 us -> 306 us (level)
  waiting for transfers between devices: 179 us -> 145 us
  blocking collectives: 56.9 us -> 89.7 us
  matrix products: 36.7 us -> 31.4 us
  starting transfers between devices: 5.16 us -> 8.71 us
  local copies, waits for them, and re-layouts: 2.4 us -> 5.81 us
    unnamed x3 -> x4, waiting for transfers between devices: 0.71 us -> 104 us
    reduce_scatter x1 -> x0, waiting for transfers between devices: 85.4 us -> none  [on_device(): lax.psum_scatter(grad_out_term[None].astype(jnp.bfloat16), 'dp', scatter_...]
    all_gather x0 -> x3, blocking collectives: none -> 69.4 us  [the longest x1 30.1 us: on_device(): lax.all_gather(slot_meta.reshape(experts, capacity, seq_count), 'expert')]
    all_to_all x2 -> x1, blocking collectives: 56.9 us -> 20.3 us  [on_device(): lax.all_to_all(hidden_blocks, 'dp', split_axis=0, concat_axis=0, tiled=True)]
    reduce_scatter x1, waiting for transfers between devices: 74.7 us -> 40.5 us  [on_device(): lax.psum_scatter(grad_in_term[None].astype(jnp.bfloat16), 'dp', scatter_d...]
    all_to_all x1, waiting for transfers between devices: 18 us -> 0.01 us  [on_device(): lax.all_to_all(outgoing, 'expert', split_axis=0, concat_axis=0, tiled=True)]
    dot_general x5 -> x8, matrix products: 18.8 us -> 12.6 us  [the longest x1 4.53 us: on_device(): jnp.dot(input_flat, weight_in[0], preferred_element_type=jnp.float32)]
    all_to_all x1, starting transfers between devices: 4.86 us -> 8.59 us  [on_device(): lax.all_to_all(outgoing, 'expert', split_axis=0, concat_axis=0, tiled=True)]
  transfers between devices with their start and end apart: 4 -> 4, of which waited for: 3 -> 2; matrix products, arithmetic and copies ran while one was open for 9% -> 2% of each run, Pallas kernels for 0% -> 0%
where the time goes in v1:
time: 306 us; the launch traced here: 305 us
  waiting for transfers between devices  145 us (47%)
  blocking collectives  89.7 us (29%)
  matrix products  31.4 us (10%)
  between operations  16.4 us (5%)
  starting transfers between devices  8.71 us (3%)
  other arithmetic  8.46 us (3%)
  local copies, waits for them, and re-layouts  5.81 us (2%)
    unnamed x4, waiting for transfers between devices  104 us
    reduce_scatter x1, waiting for transfers between devices, on_device(): lax.psum_scatter(grad_in_term[None].astype(jnp.bfloat16), 'dp', scatter_d...  40.5 us
    all_gather x1, blocking collectives, on_device(): lax.all_gather(slot_meta.reshape(experts, capacity, seq_count), 'expert')  30.1 us
    all_gather x1, blocking collectives, on_device(): lax.all_gather(delta_row.astype(jnp.bfloat16), 'dp', axis=0, tiled=True)  23.2 us
    all_to_all x1, blocking collectives, on_device(): lax.all_to_all(hidden_blocks, 'dp', split_axis=0, concat_axis=0, tiled=True)  20.3 us
    all_gather x1, blocking collectives, on_device(): delta_row = lax.all_gather(delta_seq, 'expert', axis=0, tiled=True)  16.2 us
    dot_general x1, matrix products, on_device(): lax.dot_general(input_flat, delta_pre, (((0,), (0,)), ((), ())), preferre...  11.4 us
    all_to_all x1, starting transfers between devices, on_device(): lax.all_to_all(outgoing, 'expert', split_axis=0, concat_axis=0, tiled=True)  8.59 us
  transfers between devices with their start and end apart: 4, of which 2 were waited for; matrix products, arithmetic and copies ran while one was open for 2% of the time, Pallas kernels for 0%

profile of v1, /device:TPU:32, one launch (start us, length us, event | category | flops | bytes accessed | tf_op | source)
XLA Modules:
  0.0 305.2 jit_solution(8789873288827094096)
XLA Ops:
  8.0 0.8 copy.57
  8.8 0.1 eq.101
  8.9 0.1 eq.105
  9.1 0.6 reduce-window.6
  9.7 0.2 slice_reduce_fusion
  9.9 0.1 fusion.35
  10.0 0.1 sub.31
  10.2 0.7 multiply_add_fusion.1
  10.9 1.0 fusion.57
  12.0 0.8 select_reduce_fusion.1
  12.8 0.2 fusion.30
  13.0 2.2 convolution_convert_fusion.2
  15.2 8.6 %all-to-all-start = ((bf16[16,32,768]{2,1,0:T(8,128)(2,1)}), bf16[16,32,768]{2,1,0:T(8,128)(2,1)S(1)}, u32[]{:S(2)}, u32[]{:S(2)}) async-start(bf16[16,32,768]{2,1,0:T(8,128)(2,1)} %bitcast.1), calls=%async_computation | async-start | bytes 1572864 | tf_op jit(solution)/shard_map/all_to_all | solution.py:109
  23.8 0.1 copy.61
  23.9 0.3 fusion.41
  24.2 30.1 %all-gather = f32[256,32,2]{1,2,0:T(2,128)S(1)} all-gather(f32[16,32,2]{1,2,0:T(2,128)S(1)} %fusion.41), channel_id=2, replica_groups=mesh['dp'=16,'expert'=16] {'expert'}, dimensions={0}, use_global_device_ids=true | all-gather | bytes 69632 | tf_op jit(solution)/shard_map/all_gather | solution.py:98
  54.3 0.1 broadcast_multiply_fusion
  54.4 0.1 mul.159
  54.6 4.5 %fusion.12 = f32[512,3072]{1,0:T(8,128)S(1)} fusion(bf16[512,768]{1,0:T(8,128)(2,1)S(1)} %bitcast.82, bf16[1,768,3072]{2,1,0:T(8,128)(2,1)} %param.11), kind=kOutput, calls=%fused_computation.17 | convolution fusion | flops 2415919104 | bytes 11796480 | tf_op jit(solution)/shard_map/dot_general | solution.py:111
  59.2 2.5 fusion.15
  61.6 0.7 copy-done.2
  62.3 1.3 slice-done.1
  63.6 0.9 fusion.8
  64.5 1.5 fusion.21
  66.1 0.5 all-gather.4.cloned.1.call-update
  66.7 0.6 dynamic-slice
  67.9 0.8 dynamic_slice.13
  68.7 0.2 fusion.40
  68.9 0.1 broadcast_bitcast_fusion
  69.0 103.7 %all-reduce.3.cloned.1.call-done = f32[32,768]{1,0:T(8,128)} async-done(((f32[32,768]{1,0:T(8,128)}), f32[32,768]{1,0:T(8,128)}) %all-reduce.3.cloned.1.call-update) | async-done | bytes 98320
  172.7 0.9 multiply_reduce_fusion.2
  173.6 2.7 multiply_reduce_fusion
  176.3 0.2 select_reduce_fusion
  176.5 2.9 fusion.56
  179.5 0.5 convolution_divide_fusion
  180.0 0.7 multiply_reduce_fusion.1
  180.7 0.1 multiply_bitcast_fusion
  180.7 16.2 %all-gather.1 = f32[16,2,768]{2,1,0:T(2,128)S(1)} all-gather(f32[1,2,768]{2,1,0:T(2,128)S(1)} %multiply_bitcast_fusion), channel_id=1, replica_groups=mesh['dp'=16,'expert'=16] {'expert'}, dimensions={0}, use_global_device_ids=true | all-gather | bytes 104448 | tf_op jit(solution)/shard_map/all_gather | solution.py:142
  197.0 1.4 convolution_convert_fusion.1
  198.5 11.4 %fusion.14 = bf16[1,768,3072]{2,1,0:T(8,128)(2,1)} fusion(bf16[512,768]{1,0:T(8,128)(2,1)S(1)} %bitcast.83, f32[512,3072]{1,0:T(8,128)} %copy-done.2, bf16[512,768]{1,0:T(8,128)(2,1)S(1)} %convolution_convert_fusion.1, bf16[1,3072,768]{2,1,0:T(8,128)(2,1)} %param.12), kind=kOutput, calls=%fused_computation.19 | convolution fusion | flops 4864081920 | bytes 17301504 | tf_op jit(solution)/shard_map/dot_general | solution.py:152
  209.9 0.2 reshape.113
  210.1 0.3 copy.67
  210.4 20.3 %all_to_all.10 = f32[16,32,192]{2,1,0:T(8,128)S(1)} all-to-all(f32[16,32,192]{2,1,0:T(8,128)S(1)} %bitcast.84), channel_id=1, replica_groups=mesh['dp'=16,'expert'=16] {'dp'}, dimensions={0} | all-to-all | bytes 786432 | tf_op jit(solution)/shard_map/all_to_all | solution.py:163
  230.8 23.2 %all_gather.15 = bf16[512,768]{1,0:T(8,128)(2,1)S(1)} all-gather(bf16[32,768]{1,0:T(8,128)(2,1)S(1)} %convert_element_type.99), channel_id=1, replica_groups=mesh['dp'=16,'expert'=16] {'dp'}, dimensions={0}, use_global_device_ids=true | all-gather | bytes 835584 | tf_op jit(solution)/shard_map/all_gather | solution.py:165
  253.9 0.3 fusion.58
  254.3 1.2 fusion.20
  255.4 40.5 %reduce-scatter.2.cloned.1.call-done = bf16[1,48,3072]{2,1,0:T(8,128)(2,1)} async-done(((bf16[1,768,3072]{2,1,0:T(8,128)(2,1)}), bf16[1,48,3072]{2,1,0:T(8,128)(2,1)}) %reduce-scatter.2.cloned.1.call-update) | async-done | bytes 294928 | tf_op jit(solution)/shard_map/reduce_scatter | solution.py:155
  296.0 1.8 convert_element_type.97
  (39 shorter events, 0.6 us)
Async XLA Ops:
  8.0 2.9 copy-start
  15.2 39.4 %all-to-all-start = ((bf16[16,32,768]{2,1,0:T(8,128)(2,1)}), bf16[16,32,768]{2,1,0:T(8,128)(2,1)S(1)}, u32[]{:S(2)}, u32[]{:S(2)}) async-start(bf16[16,32,768]{2,1,0:T(8,128)(2,1)} %bitcast.1), calls=%async_computation | async-start | bytes 1572864 | tf_op jit(solution)/shard_map/all_to_all | solution.py:109
  23.7 148.9 %all-reduce.3.cloned.1.call-start = ((), (), s32[]{:S(2)}) async-start(), calls=%async_computation.5 | async-start | bytes 196608
  54.6 7.7 %slice-start = ((s8[4718592]{0:T(1024)(128)(4,1)}), s8[524288]{0:T(1024)(128)(4,1)S(1)}, s32[]{:S(2)}) async-start(s8[4718592]{0:T(1024)(128)(4,1)} %bitcast.80), calls=%async_computation.6 | async-start | bytes 1048576
  59.1 3.2 %copy-start.2 = (f32[512,3072]{1,0:T(8,128)}, f32[512,3072]{1,0:T(8,128)S(1)}, u32[]{:S(2)}) copy-start(f32[512,3072]{1,0:T(8,128)S(1)} %fusion.12) | copy-start | bytes 18874372
  59.1 4.5 %slice-start.1 = ((s8[4718592]{0:T(1024)(128)(4,1)}), s8[4194304]{0:T(1024)(128)(4,1)S(1)}, s32[]{:S(2)}) async-start(s8[4718592]{0:T(1024)(128)(4,1)} %bitcast.80), calls=%async_computation.7 | async-start | bytes 8388608
  63.6 3.1 %copy-start.5 = (u32[256]{0:T(256)S(1)}, u32[256]{0:T(256)}, u32[]{:S(2)}) copy-start(u32[256]{0:T(256)} %constant.84) | copy-start | bytes 3076
  63.6 5.1 %copy-start.4 = (s32[256,16]{0,1:T(8,128)S(1)}, s32[256,16]{0,1:T(8,128)}, u32[]{:S(2)}) copy-start(s32[256,16]{0,1:T(8,128)} %param.15) | copy-start | bytes 49156
  63.6 5.2 %copy-start.3 = (bf16[128,768]{1,0:T(8,128)(2,1)S(1)}, bf16[128,768]{1,0:T(8,128)(2,1)}, u32[]{:S(2)}) copy-start(bf16[128,768]{1,0:T(8,128)(2,1)} %param.8) | copy-start | bytes 589828
  66.0 107.5 %all-gather.4.cloned.1.call-start = ((), (), s32[]{:S(2)}) async-start(), calls=%async_computation.3 | async-start | bytes 3342336 | tf_op jit(solution)/shard_map/all_gather | solution.py:124
  66.6 229.4 %reduce-scatter.2.cloned.1.call-start = ((), (), s32[]{:S(2)}) async-start(), calls=%async_computation.4 | async-start | bytes 5013504 | tf_op jit(solution)/shard_map/reduce_scatter | solution.py:155
  173.6 5.9 %copy-start.1 = (bf16[2048,768]{1,0:T(8,128)(2,1)S(1)}, bf16[2048,768]{1,0:T(8,128)(2,1)}, u32[]{:S(2)}) copy-start(bf16[2048,768]{1,0:T(8,128)(2,1)} %all-gather.4.cloned.1.call-done) | copy-start | bytes 9437188
Sparse Core Ops, SparseCore 0:
  66.1 106.4 all-reduce.2
Sparse Core Ops, SparseCore 1:
  68.9 54.3 all-gather.3
  210.0 85.9 reduce-scatter.1

commit v2 on v1

--- a/solution.py
+++ b/solution.py
@@ -67,15 +67,81 @@
     return (weighted_sum, partition, pos_vec)
 
 
+def ring_pairs(nx, ny, along_x, step):
+    pairs = []
+    for y in range(ny):
+        for x in range(nx):
+            if along_x:
+                pairs.append((y * nx + x, y * nx + (x + step) % nx))
+            else:
+                pairs.append((y * nx + x, ((y + step) % ny) * nx + x))
+    return pairs
+
+
+def take_chunk(chunks, index, count):
+    return lax.dynamic_index_in_dim(chunks, lax.rem(index + 2 * count, count), 0, keepdims=False)
+
+
+def ring_start(chunks, count, pos):
+    half = chunks.shape[-1] // 2
+    fwd, bwd = chunks[..., :half], chunks[..., half:]
+    return dict(fwd=fwd, bwd=bwd, count=count, pos=pos,
+                acc_f=take_chunk(fwd, pos - 1, count).astype(jnp.float32),
+                acc_b=take_chunk(bwd, pos + 1, count).astype(jnp.float32))
+
+
+def ring_step(state, k, fwd_pairs, bwd_pairs):
+    count, pos = state["count"], state["pos"]
+    got_f = lax.ppermute(state["acc_f"].astype(jnp.bfloat16), "dp", fwd_pairs)
+    got_b = lax.ppermute(state["acc_b"].astype(jnp.bfloat16), "dp", bwd_pairs)
+    state = dict(state)
+    state["acc_f"] = got_f.astype(jnp.float32) + take_chunk(state["fwd"], pos - 2 - k, count).astype(jnp.float32)
+    state["acc_b"] = got_b.astype(jnp.float32) + take_chunk(state["bwd"], pos + 2 + k, count).astype(jnp.float32)
+    return state
+
+
+def ring_result(state):
+    return jnp.concatenate([state["acc_f"], state["acc_b"]], axis=-1)
+
+
+def reduce_scatter_2d(partial, nx, ny, x_pos, y_pos):
+    rows = partial.shape[0] // (nx * ny)
+    width = partial.shape[1]
+    half = width // 2
+    grid = partial.reshape(ny, nx, rows, width)
+    first = jnp.transpose(grid[..., :half], (1, 0, 2, 3))
+    second = grid[..., half:]
+    x_f, x_b = ring_pairs(nx, ny, True, 1), ring_pairs(nx, ny, True, -1)
+    y_f, y_b = ring_pairs(nx, ny, False, 1), ring_pairs(nx, ny, False, -1)
+    ra = ring_start(first, nx, x_pos)
+    rb = ring_start(second, ny, y_pos)
+    for k in range(max(nx, ny) - 1):
+        if k < nx - 1:
+            ra = ring_step(ra, k, x_f, x_b)
+        if k < ny - 1:
+            rb = ring_step(rb, k, y_f, y_b)
+    ra = ring_start(ring_result(ra), ny, y_pos)
+    rb = ring_start(ring_result(rb), nx, x_pos)
+    for k in range(max(nx, ny) - 1):
+        if k < ny - 1:
+            ra = ring_step(ra, k, y_f, y_b)
+        if k < nx - 1:
+            rb = ring_step(rb, k, x_f, x_b)
+    return jnp.concatenate([ring_result(ra), ring_result(rb)], axis=-1)
+
+
 def on_device(tokens, expert_ids, router, weight_in, weight_out, premises, positive, tile_mask):
     token_count, model_width = tokens.shape
     ffn_width = weight_in.shape[2]
     experts = router.shape[1]
     expert_size = lax.axis_size("expert")
     dp_size = lax.axis_size("dp")
+    nx = 4
+    ny = dp_size // nx
     capacity = 4 * token_count // expert_size
     slot_total = experts * capacity
     seq_count = token_count // LEN
+    row_seqs = expert_size * seq_count
     dp_index = lax.axis_index("dp")
     col_index = lax.axis_index("expert")
     device = dp_index * expert_size + col_index
@@ -87,33 +153,40 @@
     combine = jnp.sum(
         jnp.where(slot_hot, gate_wts[:, :, None], jnp.zeros((), jnp.bfloat16)), axis=1
     )
+    extra = 128
     seq_hot = (
         (jnp.arange(token_count, dtype=jnp.int32) // LEN)[:, None]
-        == jnp.arange(seq_count, dtype=jnp.int32)[None, :]
-    ).astype(jnp.float32)
-    slot_meta = lax.dot_general(
-        combine.astype(jnp.float32), seq_hot, (((0,), (0,)), ((), ())),
-        precision=HIGHEST, preferred_element_type=jnp.float32,
-    )
-    meta_all = lax.all_gather(slot_meta.reshape(experts, capacity, seq_count), "expert")
-    my_meta = lax.dynamic_index_in_dim(meta_all, col_index, 1, keepdims=False)
+        == jnp.arange(extra, dtype=jnp.int32)[None, :]
+    ).astype(jnp.bfloat16)
+    payload = jnp.concatenate([tokens, seq_hot], axis=1)
+    outgoing = lax.dot_general(
+        placing, payload, (((0,), (0,)), ((), ())), preferred_element_type=jnp.float32
+    )
+    outgoing = jnp.concatenate(
+        [outgoing[:, :model_width],
+         lax.dot_general(combine, seq_hot, (((0,), (0,)), ((), ())),
+                         preferred_element_type=jnp.float32)],
+        axis=1,
+    ).astype(jnp.bfloat16)
+    outgoing = outgoing.reshape(experts, capacity, model_width + extra)
+    arrived = lax.all_to_all(outgoing, "expert", split_axis=0, concat_axis=0, tiled=True)
+    input_flat = arrived[:, :, :model_width].reshape(expert_size * capacity, model_width)
+    my_meta = arrived[:, :, model_width:model_width + seq_count].astype(jnp.float32)
     same_src = jnp.eye(expert_size, dtype=jnp.float32)
     meta_t = jnp.transpose(my_meta, (2, 0, 1))
     sel_gate = same_src[:, None, :, None] * meta_t[None, :, :, :]
-    sel_gate = sel_gate.reshape(expert_size * seq_count, expert_size * capacity)
-
-    outgoing = lax.dot_general(
-        placing, tokens, (((0,), (0,)), ((), ())), preferred_element_type=jnp.float32
-    ).astype(jnp.bfloat16)
-    outgoing = outgoing.reshape(experts, capacity, model_width)
-    arrived = lax.all_to_all(outgoing, "expert", split_axis=0, concat_axis=0, tiled=True)
-    input_flat = arrived.reshape(expert_size * capacity, model_width)
+    sel_gate = sel_gate.reshape(row_seqs, expert_size * capacity)
+
     pre_act = jnp.dot(input_flat, weight_in[0], preferred_element_type=jnp.float32)
     gelu_val, slope_flat = gelu_parts(pre_act)
     hidden = gelu_val.astype(jnp.bfloat16)
     seq_hidden = jnp.dot(sel_gate.astype(jnp.bfloat16), hidden, preferred_element_type=jnp.float32)
     moe_seq = split_dot(seq_hidden, weight_out[0], (((1,), (0,)), ((), ())))
-    moe_mine = lax.psum_scatter(moe_seq, "expert", scatter_dimension=0, tiled=True)
+    moe_back = lax.all_to_all(
+        moe_seq.reshape(expert_size, seq_count, model_width), "expert",
+        split_axis=0, concat_axis=0, tiled=True,
+    )
+    moe_mine = jnp.sum(moe_back, axis=0)
 
     token_sum = jnp.sum(tokens.astype(jnp.float32).reshape(seq_count, LEN, model_width), axis=1)
     pooled = (token_sum + moe_mine) / LEN
@@ -138,12 +211,13 @@
     delta_pooled = row_scale[:, None] * (
         delta_unit - unit_vec * jnp.sum(unit_vec * delta_unit, axis=1, keepdims=True)
     )
-    delta_seq = delta_pooled / LEN
-    delta_row = lax.all_gather(delta_seq, "expert", axis=0, tiled=True)
+    delta_seq = (delta_pooled / LEN).astype(jnp.bfloat16)
+    delta_all = lax.all_gather(delta_seq, ("dp", "expert"), axis=0, tiled=True)
+    delta_row = lax.dynamic_slice_in_dim(delta_all, dp_index * row_seqs, row_seqs)
 
     grad_flat = lax.dot_general(
-        sel_gate, delta_row, (((0,), (0,)), ((), ())),
-        precision=HIGHEST, preferred_element_type=jnp.float32,
+        sel_gate.astype(jnp.bfloat16), delta_row, (((0,), (0,)), ((), ())),
+        preferred_element_type=jnp.float32,
     ).astype(jnp.bfloat16)
     dhidden = lax.dot_general(
         grad_flat, weight_out[0], (((1,), (1,)), ((), ())), preferred_element_type=jnp.float32
@@ -151,20 +225,17 @@
     delta_pre = (dhidden * slope_flat).astype(jnp.bfloat16)
     grad_in_term = lax.dot_general(
         input_flat, delta_pre, (((0,), (0,)), ((), ())), preferred_element_type=jnp.float32
-    )
-    grad_in = lax.psum_scatter(
-        grad_in_term[None].astype(jnp.bfloat16), "dp", scatter_dimension=1, tiled=True
-    ).astype(jnp.float32)
+    ).astype(jnp.bfloat16)
+    grad_in = reduce_scatter_2d(grad_in_term, nx, ny, lax.rem(dp_index, nx), dp_index // nx)
 
     block = ffn_width // dp_size
     hidden_blocks = jnp.transpose(
-        seq_hidden.reshape(expert_size * seq_count, dp_size, block), (1, 0, 2)
+        seq_hidden.reshape(row_seqs, dp_size, block), (1, 0, 2)
     )
     hidden_cols = lax.all_to_all(hidden_blocks, "dp", split_axis=0, concat_axis=0, tiled=True)
-    hidden_cols = hidden_cols.reshape(dp_size * expert_size * seq_count, block)
-    delta_all = lax.all_gather(delta_row.astype(jnp.bfloat16), "dp", axis=0, tiled=True)
+    hidden_cols = hidden_cols.reshape(dp_size * row_seqs, block)
     grad_out = split_dot(hidden_cols, delta_all, (((0,), (0,)), ((), ())))
-    return (grad_in, grad_out[None])
+    return (grad_in[None], grad_out[None])
 
 
 def solution(mesh):

time: 306 us -> 249 us (0.81)
  waiting for transfers between devices: 145 us -> 48.1 us
  starting transfers between devices: 8.71 us -> 63.2 us
  blocking collectives: 89.7 us -> 71.1 us
  local copies, waits for them, and re-layouts: 5.81 us -> 10.8 us
    unnamed x4 -> x1, waiting for transfers between devices: 104 us -> 0.68 us
    ppermute x0 -> x24, starting transfers between devices: none -> 40.8 us  [the longest x12 33.9 us: ring_step(): got_b = lax.ppermute(state['acc_b'].astype(jnp.bfloat16), 'dp', bwd_pairs)]
    reduce_scatter x1 -> x0, waiting for transfers between devices: 40.5 us -> none  [on_device(): lax.psum_scatter(grad_in_term[None].astype(jnp.bfloat16), 'dp', scatter_d...]
    all_to_all x1, waiting for transfers between devices: 0.01 us -> 20.8 us  [on_device(): lax.all_to_all(outgoing, 'expert', split_axis=0, concat_axis=0, tiled=True)]
    all_to_all x1 -> x0, blocking collectives: 20.3 us -> none  [on_device(): lax.all_to_all(hidden_blocks, 'dp', split_axis=0, concat_axis=0, tiled=True)]
    all_to_all x0 -> x2, waiting for transfers between devices: none -> 17.4 us  [the longest x1 12.1 us: on_device(): lax.all_to_all(hidden_blocks, 'dp', split_axis=0, concat_axis=0, tiled=True)]
    all_to_all x0 -> x2, starting transfers between devices: none -> 13.8 us  [the longest x1 7.05 us: on_device(): lax.all_to_all(hidden_blocks, 'dp', split_axis=0, concat_axis=0, tiled=True)]
    ppermute x0 -> x24, waiting for transfers between devices: none -> 9.24 us  [the longest x12 9.2 us: ring_step(): got_f = lax.ppermute(state['acc_f'].astype(jnp.bfloat16), 'dp', fwd_pairs)]
  transfers between devices with their start and end apart: 4 -> 28, of which waited for: 2 -> 8; matrix products, arithmetic and copies ran while one was open for 2% -> 9% of each run, Pallas kernels for 0% -> 0%
where the time goes in v2:
time: 249 us; the launch traced here: 246 us
  blocking collectives  71.1 us (29%)
  starting transfers between devices  63.2 us (25%)
  waiting for transfers between devices  48.1 us (19%)
  matrix products  28.8 us (12%)
  between operations  14.6 us (6%)
  local copies, waits for them, and re-layouts  10.8 us (4%)
  other arithmetic  9.11 us (4%)
    all_gather x1, blocking collectives, on_device(): delta_all = lax.all_gather(delta_seq, ('dp', 'expert'), axis=0, tiled=True)  71.1 us
    ppermute x12, starting transfers between devices, ring_step(): got_b = lax.ppermute(state['acc_b'].astype(jnp.bfloat16), 'dp', bwd_pairs)  33.9 us
    all_to_all x1, waiting for transfers between devices, on_device(): lax.all_to_all(outgoing, 'expert', split_axis=0, concat_axis=0, tiled=True)  20.8 us
    all_to_all x1, waiting for transfers between devices, on_device(): lax.all_to_all(hidden_blocks, 'dp', split_axis=0, concat_axis=0, tiled=True)  12.1 us
    dot_general x1, matrix products, on_device(): lax.dot_general(input_flat, delta_pre, (((0,), (0,)), ((), ())), preferre...  11.4 us
    ppermute x12, waiting for transfers between devices, ring_step(): got_f = lax.ppermute(state['acc_f'].astype(jnp.bfloat16), 'dp', fwd_pairs)  9.2 us
    all_to_all x1, starting transfers between devices, on_device(): lax.all_to_all(outgoing, 'expert', split_axis=0, concat_axis=0, tiled=True)  8.59 us
    all_to_all x1, starting transfers between devices, on_device(): lax.all_to_all(hidden_blocks, 'dp', split_axis=0, concat_axis=0, tiled=True)  7.05 us
  transfers between devices with their start and end apart: 28, of which 8 were waited for; matrix products, arithmetic and copies ran while one was open for 9% of the time, Pallas kernels for 0%

profile of v2, /device:TPU:32, one launch (start us, length us, event | category | flops | bytes accessed | tf_op | source)
XLA Modules:
  0.0 245.9 jit_solution(216233525662895663)
XLA Ops:
  7.9 0.8 copy.70
  10.2 0.7 multiply_add_fusion.1
  10.9 1.0 fusion.85
  11.9 0.8 select_reduce_fusion.1
  13.0 1.3 fusion.38
  14.8 1.0 pad_maximum_fusion
  15.8 8.6 %all-to-all-start = ((bf16[16,32,896]{2,1,0:T(8,128)(2,1)}), bf16[16,32,896]{2,1,0:T(8,128)(2,1)S(1)}, u32[]{:S(2)}, u32[]{:S(2)}) async-start(bf16[16,32,896]{2,1,0:T(8,128)(2,1)} %pad_maximum_fusion), calls=%async_computation | async-start | bytes 1835008 | tf_op jit(solution)/shard_map/all_to_all | solution.py:172
  24.4 0.8 dynamic_slice.109
  25.4 20.8 %all-to-all-done = bf16[16,32,896]{2,1,0:T(8,128)(2,1)S(1)} async-done(((bf16[16,32,896]{2,1,0:T(8,128)(2,1)}), bf16[16,32,896]{2,1,0:T(8,128)(2,1)S(1)}, u32[]{:S(2)}, u32[]{:S(2)}) %all-to-all-start) | async-done | bytes 917536 | tf_op jit(solution)/shard_map/all_to_all | solution.py:172
  46.8 4.5 %fusion.12 = f32[512,3072]{1,0:T(8,128)S(1)} fusion(bf16[512,768]{1,0:T(8,128)(2,1)S(1)} %bitcast.183, bf16[1,768,3072]{2,1,0:T(8,128)(2,1)} %param.11), kind=kOutput, calls=%fused_computation.17 | convolution fusion | flops 2415919104 | bytes 11796480 | tf_op jit(solution)/shard_map/dot_general | solution.py:180
  51.3 2.5 %fusion.14 = f32[32,3072]{1,0:T(8,128)S(1)} fusion(bf16[32,512]{1,0:T(8,128)(2,1)S(1)} %convert_element_type.309, f32[512,3072]{1,0:T(8,128)S(1)} %fusion.12), kind=kOutput, calls=%fused_computation.19 | convolution fusion | flops 114819072 | bytes 6717440 | tf_op jit(solution)/shard_map/dot_general | solution.py:183
  54.5 1.3 slice-done.1
  55.8 0.9 fusion.8
  56.7 0.9 fusion.20
  58.3 6.8 %all-to-all-start.1 = ((f32[16,2,768]{2,1,0:T(2,128)}), f32[16,2,768]{2,1,0:T(2,128)S(1)}, u32[]{:S(2)}, u32[]{:S(2)}) async-start(f32[16,2,768]{2,1,0:T(2,128)} %reshape.141), calls=%async_computation.1 | async-start | bytes 196608 | tf_op jit(solution)/shard_map/all_to_all | solution.py:185
  65.4 1.1 copy.88
  66.5 5.3 %all-to-all-done.1 = f32[16,2,768]{2,1,0:T(2,128)S(1)} async-done(((f32[16,2,768]{2,1,0:T(2,128)}), f32[16,2,768]{2,1,0:T(2,128)S(1)}, u32[]{:S(2)}, u32[]{:S(2)}) %all-to-all-start.1) | async-done | bytes 98336 | tf_op jit(solution)/shard_map/all_to_all | solution.py:185
  71.8 7.0 %all-to-all-start.2 = ((f32[16,32,192]{2,1,0:T(8,128)}), f32[16,32,192]{2,1,0:T(8,128)S(1)}, u32[]{:S(2)}, u32[]{:S(2)}) async-start(f32[16,32,192]{2,1,0:T(8,128)} %bitcast.178), calls=%async_computation.2 | async-start | bytes 1048576 | tf_op jit(solution)/shard_map/all_to_all | solution.py:235
  79.1 12.1 %all-to-all-done.2 = f32[16,32,192]{2,1,0:T(8,128)S(1)} async-done(((f32[16,32,192]{2,1,0:T(8,128)}), f32[16,32,192]{2,1,0:T(8,128)S(1)}, u32[]{:S(2)}, u32[]{:S(2)}) %all-to-all-start.2) | async-done | bytes 393248 | tf_op jit(solution)/shard_map/all_to_all | solution.py:235
  91.2 2.7 %multiply_reduce_fusion = f32[2048]{0:T(1024)S(1)} fusion(bf16[2048,768]{1,0:T(8,128)(2,1)} %all-gather.3.cloned.1.call-done), kind=kLoop, calls=%fused_computation.9 | loop fusion | flops 4716544 | bytes 3153920 | tf_op jit(solution)/shard_map/reduce_sum | solution.py:198
  94.2 2.9 %fusion.84 = (f32[2]{0:T(128)S(1)}, f32[2,2048]{1,0:T(2,128)S(1)}) fusion(f32[2048]{0:T(1024)S(1)} %get-tuple-element.13, bf16[2048,768]{1,0:T(8,128)(2,1)} %all-gather.3.cloned.1.call-done, f32[2,768]{1,0:T(2,128)S(1)} %get-tuple-element.7, f32[2]{0:T(128)S(1)} %get-tuple-element.15, s32[2]{0:T(128)S(1)} %dynamic_slice.109, ...), kind=kOutput, calls=%fused_computation.163 | convolution fusion | flops 6315006 | bytes 3178520 | tf_op jit(solution)/shard_map/dot_general | solution.py:51
  98.4 71.1 %all-gather = bf16[256,2,768]{2,1,0:T(2,128)(2,1)S(1)} all-gather(bf16[1,2,768]{2,1,0:T(2,128)(2,1)S(1)} %fusion.70), channel_id=1, replica_groups=mesh['dp'=16,'expert'=16] {'dp','expert'}, dimensions={0}, use_global_device_ids=true | all-gather | bytes 789504 | tf_op jit(solution)/shard_map/all_gather | solution.py:215
  170.2 11.4 %convolution_convert_fusion = bf16[768,3072]{1,0:T(8,128)(2,1)} fusion(bf16[512,768]{1,0:T(8,128)(2,1)S(1)} %bitcast.184, f32[512,3072]{1,0:T(8,128)} %copy-done.2, bf16[512,768]{1,0:T(8,128)(2,1)S(1)} %convolution_convert_fusion.1, bf16[1,3072,768]{2,1,0:T(8,128)(2,1)} %param.12), kind=kOutput, calls=%fused_computation.11 | convolution fusion | flops 4864081920 | bytes 17301504 | tf_op jit(solution)/shard_map/dot_general | solution.py:226
  181.6 2.0 slice_bitcast_fusion
  183.5 1.1 copy-done.3
  185.4 1.2 collective-permute-start
  186.7 2.1 collective-permute-start.6
  188.8 1.3 collective-permute-start.12
  190.1 2.1 collective-permute-start.18
  192.2 1.2 fusion.19
  193.4 2.6 %collective-permute-done = bf16[4,48,768]{2,1,0:T(8,128)(2,1)S(1)} collective-permute-done((bf16[4,48,768]{2,1,0:T(8,128)(2,1)S(1)}, bf16[4,48,768]{2,1,0:T(8,128)(2,1)S(1)}, u32[]{:S(2)}, u32[]{:S(2)}) %collective-permute-start) | collective-permute-done | bytes 294944 | tf_op jit(solution)/shard_map/ppermute | solution.py:95
  196.2 3.3 %collective-permute-start.7 = (bf16[4,48,768]{2,1,0:T(8,128)(2,1)S(1)}, bf16[4,48,768]{2,1,0:T(8,128)(2,1)S(1)}, u32[]{:S(2)}, u32[]{:S(2)}) collective-permute-start(bf16[4,48,768]{2,1,0:T(8,128)(2,1)S(1)} %fusion.30), channel_id=1, source_target_pairs={{0,48},{16,0},{32,16},{48,32},{64,112},{80,64},{96,80},{112,96},{1... | collective-permute-start | bytes 884744 | tf_op jit(solution)/shard_map/ppermute | solution.py:96
  199.6 1.3 collective-permute-start.13
  201.0 2.4 collective-permute-start.19
  203.3 2.4 collective-permute-done.1
  206.1 3.3 %collective-permute-start.8 = (bf16[4,48,768]{2,1,0:T(8,128)(2,1)S(1)}, bf16[4,48,768]{2,1,0:T(8,128)(2,1)S(1)}, u32[]{:S(2)}, u32[]{:S(2)}) collective-permute-start(bf16[4,48,768]{2,1,0:T(8,128)(2,1)S(1)} %fusion.29), channel_id=1, source_target_pairs={{0,48},{16,0},{32,16},{48,32},{64,112},{80,64},{96,80},{112,96},{1... | collective-permute-start | bytes 884744 | tf_op jit(solution)/shard_map/ppermute | solution.py:96
  209.4 1.2 collective-permute-start.14
  210.8 2.1 collective-permute-start.20
  212.9 1.8 collective-permute-done.2
  214.8 1.2 collective-permute-start.3
  216.2 2.2 collective-permute-start.9
  218.8 3.3 %collective-permute-start.21 = (bf16[48,768]{1,0:T(8,128)(2,1)S(1)}, bf16[48,768]{1,0:T(8,128)(2,1)S(1)}, u32[]{:S(2)}, u32[]{:S(2)}) collective-permute-start(bf16[48,768]{1,0:T(8,128)(2,1)S(1)} %fusion.55), channel_id=1, source_target_pairs={{0,48},{16,0},{32,16},{48,32},{64,112},{80,64},{96,80},{112,96},{1... | collective-permute-start | bytes 221192 | tf_op jit(solution)/shard_map/ppermute | solution.py:96
  222.3 3.3 %collective-permute-start.10 = (bf16[48,768]{1,0:T(8,128)(2,1)S(1)}, bf16[48,768]{1,0:T(8,128)(2,1)S(1)}, u32[]{:S(2)}, u32[]{:S(2)}) collective-permute-start(bf16[48,768]{1,0:T(8,128)(2,1)S(1)} %fusion.47), channel_id=1, source_target_pairs={{0,192},{16,208},{32,224},{48,240},{64,0},{80,16},{96,32},{112,48}... | collective-permute-start | bytes 221192 | tf_op jit(solution)/shard_map/ppermute | solution.py:96
  225.7 3.3 %collective-permute-start.22 = (bf16[48,768]{1,0:T(8,128)(2,1)S(1)}, bf16[48,768]{1,0:T(8,128)(2,1)S(1)}, u32[]{:S(2)}, u32[]{:S(2)}) collective-permute-start(bf16[48,768]{1,0:T(8,128)(2,1)S(1)} %fusion.43), channel_id=1, source_target_pairs={{0,48},{16,0},{32,16},{48,32},{64,112},{80,64},{96,80},{112,96},{1... | collective-permute-start | bytes 221192 | tf_op jit(solution)/shard_map/ppermute | solution.py:96
  229.1 3.3 %collective-permute-start.11 = (bf16[48,768]{1,0:T(8,128)(2,1)S(1)}, bf16[48,768]{1,0:T(8,128)(2,1)S(1)}, u32[]{:S(2)}, u32[]{:S(2)}) collective-permute-start(bf16[48,768]{1,0:T(8,128)(2,1)S(1)} %fusion.46), channel_id=1, source_target_pairs={{0,192},{16,208},{32,224},{48,240},{64,0},{80,16},{96,32},{112,48}... | collective-permute-start | bytes 221192 | tf_op jit(solution)/shard_map/ppermute | solution.py:96
  232.6 3.3 %collective-permute-start.23 = (bf16[48,768]{1,0:T(8,128)(2,1)S(1)}, bf16[48,768]{1,0:T(8,128)(2,1)S(1)}, u32[]{:S(2)}, u32[]{:S(2)}) collective-permute-start(bf16[48,768]{1,0:T(8,128)(2,1)S(1)} %fusion.42), channel_id=1, source_target_pairs={{0,48},{16,0},{32,16},{48,32},{64,112},{80,64},{96,80},{112,96},{1... | collective-permute-start | bytes 221192 | tf_op jit(solution)/shard_map/ppermute | solution.py:96
  235.9 2.2 collective-permute-done.17
  238.2 0.9 maximum_bitcast_fusion
  (121 shorter events, 10.6 us)
Async XLA Ops:
  7.2 3.7 %copy-start = (bf16[768,16]{0,1:T(8,128)(2,1)S(1)}, bf16[768,16]{0,1:T(8,128)(2,1)}, u32[]{:S(2)}) copy-start(bf16[768,16]{0,1:T(8,128)(2,1)} %param.10) | copy-start | bytes 73732
  7.2 18.2 %copy-start.4 = (bf16[128,768]{1,0:T(8,128)(2,1)S(1)}, bf16[128,768]{1,0:T(8,128)(2,1)}, u32[]{:S(2)}) copy-start(bf16[128,768]{1,0:T(8,128)(2,1)} %param.8) | copy-start | bytes 589828
  7.2 18.0 %copy-start.5 = (s32[256,16]{0,1:T(8,128)S(1)}, s32[256,16]{0,1:T(8,128)}, u32[]{:S(2)}) copy-start(s32[256,16]{0,1:T(8,128)} %param.15) | copy-start | bytes 49156
  7.2 84.0 %all-gather.3.cloned.1.call-start = ((), (), s32[]{:S(2)}) async-start(), calls=%async_computation.3 | async-start | bytes 3342336 | tf_op jit(solution)/shard_map/all_gather | solution.py:197
  15.8 30.4 %all-to-all-start = ((bf16[16,32,896]{2,1,0:T(8,128)(2,1)}), bf16[16,32,896]{2,1,0:T(8,128)(2,1)S(1)}, u32[]{:S(2)}, u32[]{:S(2)}) async-start(bf16[16,32,896]{2,1,0:T(8,128)(2,1)} %pad_maximum_fusion), calls=%async_computation | async-start | bytes 1835008 | tf_op jit(solution)/shard_map/all_to_all | solution.py:172
  46.8 7.8 %slice-start = ((s8[4718592]{0:T(1024)(128)(4,1)}), s8[524288]{0:T(1024)(128)(4,1)S(1)}, s32[]{:S(2)}) async-start(s8[4718592]{0:T(1024)(128)(4,1)} %bitcast.179), calls=%async_computation.4 | async-start | bytes 1048576
  51.3 3.2 %copy-start.2 = (f32[512,3072]{1,0:T(8,128)}, f32[512,3072]{1,0:T(8,128)S(1)}, u32[]{:S(2)}) copy-start(f32[512,3072]{1,0:T(8,128)S(1)} %fusion.12) | copy-start | bytes 18874372
  51.3 4.5 %slice-start.1 = ((s8[4718592]{0:T(1024)(128)(4,1)}), s8[4194304]{0:T(1024)(128)(4,1)S(1)}, s32[]{:S(2)}) async-start(s8[4718592]{0:T(1024)(128)(4,1)} %bitcast.179), calls=%async_computation.5 | async-start | bytes 8388608
  58.3 13.5 %all-to-all-start.1 = ((f32[16,2,768]{2,1,0:T(2,128)}), f32[16,2,768]{2,1,0:T(2,128)S(1)}, u32[]{:S(2)}, u32[]{:S(2)}) async-start(f32[16,2,768]{2,1,0:T(2,128)} %reshape.141), calls=%async_computation.1 | async-start | bytes 196608 | tf_op jit(solution)/shard_map/all_to_all | solution.py:185
  71.8 19.3 %all-to-all-start.2 = ((f32[16,32,192]{2,1,0:T(8,128)}), f32[16,32,192]{2,1,0:T(8,128)S(1)}, u32[]{:S(2)}, u32[]{:S(2)}) async-start(f32[16,32,192]{2,1,0:T(8,128)} %bitcast.178), calls=%async_computation.2 | async-start | bytes 1048576 | tf_op jit(solution)/shard_map/all_to_all | solution.py:235
  91.2 5.9 %copy-start.1 = (bf16[2048,768]{1,0:T(8,128)(2,1)S(1)}, bf16[2048,768]{1,0:T(8,128)(2,1)}, u32[]{:S(2)}) copy-start(bf16[2048,768]{1,0:T(8,128)(2,1)} %all-gather.3.cloned.1.call-done) | copy-start | bytes 9437188
  181.6 3.0 %copy-start.3 = (bf16[768,3072]{1,0:T(8,128)(2,1)S(1)}, bf16[768,3072]{1,0:T(8,128)(2,1)}, u32[]{:S(2)}) copy-start(bf16[768,3072]{1,0:T(8,128)(2,1)} %convolution_convert_fusion) | copy-start | bytes 14155780
  185.4 10.6 %collective-permute-start = (bf16[4,48,768]{2,1,0:T(8,128)(2,1)S(1)}, bf16[4,48,768]{2,1,0:T(8,128)(2,1)S(1)}, u32[]{:S(2)}, u32[]{:S(2)}) collective-permute-start(bf16[4,48,768]{2,1,0:T(8,128)(2,1)S(1)} %dynamic-slice_bitcast_fusion.3), channel_id=1, source_target_pairs={{0,16},{16,32},{32,48},{48,0},{64,80},{80,96},{96,112},{112,64},{1... | collective-permute-start | bytes 884744 | tf_op jit(solution)/shard_map/ppermute | solution.py:95
  186.7 9.5 %collective-permute-start.6 = (bf16[4,48,768]{2,1,0:T(8,128)(2,1)S(1)}, bf16[4,48,768]{2,1,0:T(8,128)(2,1)S(1)}, u32[]{:S(2)}, u32[]{:S(2)}) collective-permute-start(bf16[4,48,768]{2,1,0:T(8,128)(2,1)S(1)} %dynamic-slice_bitcast_fusion.2), channel_id=1, source_target_pairs={{0,48},{16,0},{32,16},{48,32},{64,112},{80,64},{96,80},{112,96},{1... | collective-permute-start | bytes 884744 | tf_op jit(solution)/shard_map/ppermute | solution.py:96
  188.8 10.7 %collective-permute-start.12 = (bf16[4,48,768]{2,1,0:T(8,128)(2,1)S(1)}, bf16[4,48,768]{2,1,0:T(8,128)(2,1)S(1)}, u32[]{:S(2)}, u32[]{:S(2)}) collective-permute-start(bf16[4,48,768]{2,1,0:T(8,128)(2,1)S(1)} %dynamic-slice_bitcast_fusion.1), channel_id=1, source_target_pairs={{0,64},{16,80},{32,96},{48,112},{64,128},{80,144},{96,160},{112,17... | collective-permute-start | bytes 884744 | tf_op jit(solution)/shard_map/ppermute | solution.py:95
  190.1 10.8 %collective-permute-start.18 = (bf16[4,48,768]{2,1,0:T(8,128)(2,1)S(1)}, bf16[4,48,768]{2,1,0:T(8,128)(2,1)S(1)}, u32[]{:S(2)}, u32[]{:S(2)}) collective-permute-start(bf16[4,48,768]{2,1,0:T(8,128)(2,1)S(1)} %dynamic-slice_bitcast_fusion), channel_id=1, source_target_pairs={{0,192},{16,208},{32,224},{48,240},{64,0},{80,16},{96,32},{112,48}... | collective-permute-start | bytes 884744 | tf_op jit(solution)/shard_map/ppermute | solution.py:96
  196.1 9.7 %collective-permute-start.1 = (bf16[4,48,768]{2,1,0:T(8,128)(2,1)S(1)}, bf16[4,48,768]{2,1,0:T(8,128)(2,1)S(1)}, u32[]{:S(2)}, u32[]{:S(2)}) collective-permute-start(bf16[4,48,768]{2,1,0:T(8,128)(2,1)S(1)} %fusion.32), channel_id=1, source_target_pairs={{0,16},{16,32},{32,48},{48,0},{64,80},{80,96},{96,112},{112,64},{1... | collective-permute-start | bytes 884744 | tf_op jit(solution)/shard_map/ppermute | solution.py:95
  196.2 9.7 %collective-permute-start.7 = (bf16[4,48,768]{2,1,0:T(8,128)(2,1)S(1)}, bf16[4,48,768]{2,1,0:T(8,128)(2,1)S(1)}, u32[]{:S(2)}, u32[]{:S(2)}) collective-permute-start(bf16[4,48,768]{2,1,0:T(8,128)(2,1)S(1)} %fusion.30), channel_id=1, source_target_pairs={{0,48},{16,0},{32,16},{48,32},{64,112},{80,64},{96,80},{112,96},{1... | collective-permute-start | bytes 884744 | tf_op jit(solution)/shard_map/ppermute | solution.py:96
  199.6 9.7 %collective-permute-start.13 = (bf16[4,48,768]{2,1,0:T(8,128)(2,1)S(1)}, bf16[4,48,768]{2,1,0:T(8,128)(2,1)S(1)}, u32[]{:S(2)}, u32[]{:S(2)}) collective-permute-start(bf16[4,48,768]{2,1,0:T(8,128)(2,1)S(1)} %fusion.28), channel_id=1, source_target_pairs={{0,64},{16,80},{32,96},{48,112},{64,128},{80,144},{96,160},{112,17... | collective-permute-start | bytes 884744 | tf_op jit(solution)/shard_map/ppermute | solution.py:95
  201.0 9.7 %collective-permute-start.19 = (bf16[4,48,768]{2,1,0:T(8,128)(2,1)S(1)}, bf16[4,48,768]{2,1,0:T(8,128)(2,1)S(1)}, u32[]{:S(2)}, u32[]{:S(2)}) collective-permute-start(bf16[4,48,768]{2,1,0:T(8,128)(2,1)S(1)} %fusion.26), channel_id=1, source_target_pairs={{0,192},{16,208},{32,224},{48,240},{64,0},{80,16},{96,32},{112,48}... | collective-permute-start | bytes 884744 | tf_op jit(solution)/shard_map/ppermute | solution.py:96
  205.9 8.9 %collective-permute-start.2 = (bf16[4,48,768]{2,1,0:T(8,128)(2,1)S(1)}, bf16[4,48,768]{2,1,0:T(8,128)(2,1)S(1)}, u32[]{:S(2)}, u32[]{:S(2)}) collective-permute-start(bf16[4,48,768]{2,1,0:T(8,128)(2,1)S(1)} %fusion.31), channel_id=1, source_target_pairs={{0,16},{16,32},{32,48},{48,0},{64,80},{80,96},{96,112},{112,64},{1... | collective-permute-start | bytes 884744 | tf_op jit(solution)/shard_map/ppermute | solution.py:95
  206.1 10.0 %collective-permute-start.8 = (bf16[4,48,768]{2,1,0:T(8,128)(2,1)S(1)}, bf16[4,48,768]{2,1,0:T(8,128)(2,1)S(1)}, u32[]{:S(2)}, u32[]{:S(2)}) collective-permute-start(bf16[4,48,768]{2,1,0:T(8,128)(2,1)S(1)} %fusion.29), channel_id=1, source_target_pairs={{0,48},{16,0},{32,16},{48,32},{64,112},{80,64},{96,80},{112,96},{1... | collective-permute-start | bytes 884744 | tf_op jit(solution)/shard_map/ppermute | solution.py:96
  209.4 9.1 %collective-permute-start.14 = (bf16[4,48,768]{2,1,0:T(8,128)(2,1)S(1)}, bf16[4,48,768]{2,1,0:T(8,128)(2,1)S(1)}, u32[]{:S(2)}, u32[]{:S(2)}) collective-permute-start(bf16[4,48,768]{2,1,0:T(8,128)(2,1)S(1)} %fusion.27), channel_id=1, source_target_pairs={{0,64},{16,80},{32,96},{48,112},{64,128},{80,144},{96,160},{112,17... | collective-permute-start | bytes 884744 | tf_op jit(solution)/shard_map/ppermute | solution.py:95
  210.8 7.9 %collective-permute-start.20 = (bf16[4,48,768]{2,1,0:T(8,128)(2,1)S(1)}, bf16[4,48,768]{2,1,0:T(8,128)(2,1)S(1)}, u32[]{:S(2)}, u32[]{:S(2)}) collective-permute-start(bf16[4,48,768]{2,1,0:T(8,128)(2,1)S(1)} %fusion.25), channel_id=1, source_target_pairs={{0,192},{16,208},{32,224},{48,240},{64,0},{80,16},{96,32},{112,48}... | collective-permute-start | bytes 884744 | tf_op jit(solution)/shard_map/ppermute | solution.py:96
  214.8 7.3 %collective-permute-start.3 = (bf16[48,768]{1,0:T(8,128)(2,1)S(1)}, bf16[48,768]{1,0:T(8,128)(2,1)S(1)}, u32[]{:S(2)}, u32[]{:S(2)}) collective-permute-start(bf16[48,768]{1,0:T(8,128)(2,1)S(1)} %fusion.52), channel_id=1, source_target_pairs={{0,64},{16,80},{32,96},{48,112},{64,128},{80,144},{96,160},{112,17... | collective-permute-start | bytes 221192 | tf_op jit(solution)/shard_map/ppermute | solution.py:95
  216.2 6.1 %collective-permute-start.9 = (bf16[48,768]{1,0:T(8,128)(2,1)S(1)}, bf16[48,768]{1,0:T(8,128)(2,1)S(1)}, u32[]{:S(2)}, u32[]{:S(2)}) collective-permute-start(bf16[48,768]{1,0:T(8,128)(2,1)S(1)} %fusion.53), channel_id=1, source_target_pairs={{0,192},{16,208},{32,224},{48,240},{64,0},{80,16},{96,32},{112,48}... | collective-permute-start | bytes 221192 | tf_op jit(solution)/shard_map/ppermute | solution.py:96
  218.6 6.9 %collective-permute-start.15 = (bf16[48,768]{1,0:T(8,128)(2,1)S(1)}, bf16[48,768]{1,0:T(8,128)(2,1)S(1)}, u32[]{:S(2)}, u32[]{:S(2)}) collective-permute-start(bf16[48,768]{1,0:T(8,128)(2,1)S(1)} %fusion.54), channel_id=1, source_target_pairs={{0,16},{16,32},{32,48},{48,0},{64,80},{80,96},{96,112},{112,64},{1... | collective-permute-start | bytes 221192 | tf_op jit(solution)/shard_map/ppermute | solution.py:95
  218.8 6.8 %collective-permute-start.21 = (bf16[48,768]{1,0:T(8,128)(2,1)S(1)}, bf16[48,768]{1,0:T(8,128)(2,1)S(1)}, u32[]{:S(2)}, u32[]{:S(2)}) collective-permute-start(bf16[48,768]{1,0:T(8,128)(2,1)S(1)} %fusion.55), channel_id=1, source_target_pairs={{0,48},{16,0},{32,16},{48,32},{64,112},{80,64},{96,80},{112,96},{1... | collective-permute-start | bytes 221192 | tf_op jit(solution)/shard_map/ppermute | solution.py:96
  222.1 6.9 %collective-permute-start.4 = (bf16[48,768]{1,0:T(8,128)(2,1)S(1)}, bf16[48,768]{1,0:T(8,128)(2,1)S(1)}, u32[]{:S(2)}, u32[]{:S(2)}) collective-permute-start(bf16[48,768]{1,0:T(8,128)(2,1)S(1)} %fusion.49), channel_id=1, source_target_pairs={{0,64},{16,80},{32,96},{48,112},{64,128},{80,144},{96,160},{112,17... | collective-permute-start | bytes 221192 | tf_op jit(solution)/shard_map/ppermute | solution.py:95
  222.3 6.8 %collective-permute-start.10 = (bf16[48,768]{1,0:T(8,128)(2,1)S(1)}, bf16[48,768]{1,0:T(8,128)(2,1)S(1)}, u32[]{:S(2)}, u32[]{:S(2)}) collective-permute-start(bf16[48,768]{1,0:T(8,128)(2,1)S(1)} %fusion.47), channel_id=1, source_target_pairs={{0,192},{16,208},{32,224},{48,240},{64,0},{80,16},{96,32},{112,48}... | collective-permute-start | bytes 221192 | tf_op jit(solution)/shard_map/ppermute | solution.py:96
  225.6 6.9 %collective-permute-start.16 = (bf16[48,768]{1,0:T(8,128)(2,1)S(1)}, bf16[48,768]{1,0:T(8,128)(2,1)S(1)}, u32[]{:S(2)}, u32[]{:S(2)}) collective-permute-start(bf16[48,768]{1,0:T(8,128)(2,1)S(1)} %fusion.45), channel_id=1, source_target_pairs={{0,16},{16,32},{32,48},{48,0},{64,80},{80,96},{96,112},{112,64},{1... | collective-permute-start | bytes 221192 | tf_op jit(solution)/shard_map/ppermute | solution.py:95
  225.7 6.8 %collective-permute-start.22 = (bf16[48,768]{1,0:T(8,128)(2,1)S(1)}, bf16[48,768]{1,0:T(8,128)(2,1)S(1)}, u32[]{:S(2)}, u32[]{:S(2)}) collective-permute-start(bf16[48,768]{1,0:T(8,128)(2,1)S(1)} %fusion.43), channel_id=1, source_target_pairs={{0,48},{16,0},{32,16},{48,32},{64,112},{80,64},{96,80},{112,96},{1... | collective-permute-start | bytes 221192 | tf_op jit(solution)/shard_map/ppermute | solution.py:96
  229.0 6.9 %collective-permute-start.5 = (bf16[48,768]{1,0:T(8,128)(2,1)S(1)}, bf16[48,768]{1,0:T(8,128)(2,1)S(1)}, u32[]{:S(2)}, u32[]{:S(2)}) collective-permute-start(bf16[48,768]{1,0:T(8,128)(2,1)S(1)} %fusion.48), channel_id=1, source_target_pairs={{0,64},{16,80},{32,96},{48,112},{64,128},{80,144},{96,160},{112,17... | collective-permute-start | bytes 221192 | tf_op jit(solution)/shard_map/ppermute | solution.py:95
  229.1 6.8 %collective-permute-start.11 = (bf16[48,768]{1,0:T(8,128)(2,1)S(1)}, bf16[48,768]{1,0:T(8,128)(2,1)S(1)}, u32[]{:S(2)}, u32[]{:S(2)}) collective-permute-start(bf16[48,768]{1,0:T(8,128)(2,1)S(1)} %fusion.46), channel_id=1, source_target_pairs={{0,192},{16,208},{32,224},{48,240},{64,0},{80,16},{96,32},{112,48}... | collective-permute-start | bytes 221192 | tf_op jit(solution)/shard_map/ppermute | solution.py:96
  232.5 5.6 %collective-permute-start.17 = (bf16[48,768]{1,0:T(8,128)(2,1)S(1)}, bf16[48,768]{1,0:T(8,128)(2,1)S(1)}, u32[]{:S(2)}, u32[]{:S(2)}) collective-permute-start(bf16[48,768]{1,0:T(8,128)(2,1)S(1)} %fusion.44), channel_id=1, source_target_pairs={{0,16},{16,32},{32,48},{48,0},{64,80},{80,96},{96,112},{112,64},{1... | collective-permute-start | bytes 221192 | tf_op jit(solution)/shard_map/ppermute | solution.py:95
  232.6 5.5 %collective-permute-start.23 = (bf16[48,768]{1,0:T(8,128)(2,1)S(1)}, bf16[48,768]{1,0:T(8,128)(2,1)S(1)}, u32[]{:S(2)}, u32[]{:S(2)}) collective-permute-start(bf16[48,768]{1,0:T(8,128)(2,1)S(1)} %fusion.42), channel_id=1, source_target_pairs={{0,48},{16,0},{32,16},{48,32},{64,112},{80,64},{96,80},{112,96},{1... | collective-permute-start | bytes 221192 | tf_op jit(solution)/shard_map/ppermute | solution.py:96
Sparse Core Ops, SparseCore 0:
  10.4 55.3 all-gather.2
